TPU v7x, 128 devices: a whole 4x4x4 slice. The times are simulated.
128 devices in a mesh: seq: 16 (over x, y), resp: 8 (over z, core).
Axes of the slice: x: 4, y: 4, z: 4, core: 2. Of those that a mesh axis runs over, the one named last changes fastest.
Arguments:
- prompt_keys: bfloat16 [2, 2048, 1024], P(None, 'seq'), may hold values from -6.1 to 6.1
- prompt_values: bfloat16 [2, 2048, 1024], P(None, 'seq'), may hold values from -6 to 6
- resp_query: bfloat16 [16, 1024, 8192], P('resp', None, 'seq'), may hold values from -121 to 121
- resp_keys: bfloat16 [16, 1024, 1024], P('resp'), may hold values from -6 to 6
- resp_values: bfloat16 [16, 1024, 1024], P('resp'), may hold values from -6 to 6
- prompt_x: bfloat16 [2, 2048, 16384], P(None, 'seq', 'resp'), may hold values from -6 to 6
- prompt_dt: float32 [2, 256, 2048], P(None, 'resp', 'seq'), may hold values from 0 to 0.5, as said below
- prompt_b: bfloat16 [2, 2048, 128], P(None, 'seq'), may hold values from -6 to 6
- prompt_c: bfloat16 [2, 2048, 128], P(None, 'seq'), may hold values from -0.5 to 0.5
- resp_x: bfloat16 [16, 1024, 16384], P('resp', None, 'seq'), may hold values from -6 to 6
- resp_dt: float32 [16, 256, 1024], P('resp', 'seq'), may hold values from 0 to 0.5, as said below
- resp_b: bfloat16 [16, 1024, 128], P('resp'), may hold values from -6 to 6
- resp_c: bfloat16 [16, 1024, 128], P('resp'), may hold values from -0.5 to 0.5
- ssm_rate: float32 [256], replicated, may hold values from 0.7 to 1.4
- resp_group: int32 [16], P('resp'), may hold values from 0 to 1
- resp_len: int32 [16], P('resp'), may hold values from 1 to 1024, 10240 in all
Outputs:
- resp_attn_out: bfloat16 [16, 1024, 8192], P('resp', None, 'seq')
- resp_ssm_out: bfloat16 [16, 1024, 16384], P('resp', None, 'seq')
- prompt_ssm_out: bfloat16 [2, 2048, 16384], P(None, 'seq', 'resp')
Inputs may be any that keep to these rules, and one draw needn't show every extreme that they name: `prompt_dt`: positive step sizes. `resp_dt`: positive step sizes.
All inputs are finite; a program needn't handle non-finite values. No bound on the sum of `resp_len` on one device may be relied on, other than what follows from the above.
Results may differ from a plain program's by a relative error of at most 0.0048.
Values may be sent and summed in bfloat16 or wider, within the bound.
No kernel may reach another device: no remote copies, remote signals or barrier semaphores. Data moves between devices by JAX's collectives and lax.ppermute only.
A program may use at most 192 MiB of HBM per device.

v0:
```python
import math

import jax
import jax.numpy as jnp
from jax import lax
from jax.sharding import PartitionSpec as P

HDIM = 128
SP = 64
NST = 128
QS = 128


EPS = 1e-05


def from_behind(block, axis, distance):
    devices = range(lax.axis_size(axis))
    route = [(i - distance, i) for i in devices if i - distance in devices]
    return lax.ppermute(block, axis, route)


def broadcast(value, axis, source):
    kept = jnp.where(lax.axis_index(axis) == source, value, 0).astype(value.dtype)
    return lax.psum(kept, axis)


def block_pass(inputs, steps, b_rows, c_rows, rates, state):
    exponent = jnp.cumsum(-steps * rates[:, None], axis=1)
    width = inputs.shape[0]
    lower = lax.broadcasted_iota(jnp.int32, (width, width), 0) >= lax.broadcasted_iota(
        jnp.int32, (width, width), 1
    )
    spread = jnp.where(lower[None], exponent[:, :, None] - exponent[:, None, :], -jnp.inf)
    gram = jnp.dot(c_rows, b_rows.T, preferred_element_type=jnp.float32)
    mixing = (jnp.exp(spread) * gram[None] * steps[:, None, :]).astype(jnp.bfloat16)
    local = jnp.einsum("hts,shp->thp", mixing, inputs, preferred_element_type=jnp.float32)
    carried = jnp.einsum(
        "tn,hpn->thp", c_rows.astype(jnp.float32), state, precision=lax.Precision.HIGHEST
    )
    output = local + carried * jnp.exp(exponent).T[:, :, None]
    last = exponent[:, -1]
    weighted = (
        inputs.astype(jnp.float32) * (jnp.exp(last[:, None] - exponent) * steps).T[:, :, None]
    ).astype(jnp.bfloat16)
    fresh = jnp.einsum("thp,tn->hpn", weighted, b_rows, preferred_element_type=jnp.float32)
    return (output, jnp.exp(last)[:, None, None] * state + fresh, exponent)


def sequence_pass(inputs, steps, b_rows, c_rows, rates):
    window_extent = inputs.shape[0]
    heads = steps.shape[0]
    blocks = window_extent // QS
    xs = inputs.reshape(blocks, QS, heads, SP)
    ss = steps.reshape(heads, blocks, QS).transpose(1, 0, 2)
    bs = b_rows.reshape(blocks, QS, NST)
    cs = c_rows.reshape(blocks, QS, NST)

    def advance(carry, block):
        state, offset = carry
        out, state_next, exponent = block_pass(block[0], block[1], block[2], block[3], rates, state)
        return ((state_next, offset + exponent[:, -1]), (out, offset[:, None] + exponent))

    start = (jnp.zeros((heads, SP, NST), jnp.float32), jnp.zeros((heads,), jnp.float32))
    (final, total), (outs, decays_to) = lax.scan(advance, start, (xs, ss, bs, cs))
    decays_to = decays_to.transpose(1, 0, 2).reshape(heads, window_extent)
    return (outs.reshape(window_extent, heads, SP), final, decays_to, total)


def head_norm(values):
    scale = lax.rsqrt(jnp.mean(values * values, axis=-1, keepdims=True) + EPS)
    return (values * scale).reshape(values.shape[0], -1)


def linkage_merge(earlier, later):
    return (earlier[0] * later[0], later[0][:, :, None, None] * earlier[1] + later[1])


def body(
    prompt_keys,
    prompt_values,
    resp_query,
    resp_keys,
    resp_values,
    prompt_x,
    prompt_dt,
    prompt_b,
    prompt_c,
    resp_x,
    resp_dt,
    resp_b,
    resp_c,
    ssm_rate,
    resp_group,
    resp_len,
):
    seq_index = lax.axis_index("seq")
    resp_index = lax.axis_index("resp")
    seq_count = lax.axis_size("seq")
    prompt_count = prompt_x.shape[0]
    prompt_heads = prompt_dt.shape[1]
    resp_heads = resp_dt.shape[1]
    responses_here = resp_x.shape[0]
    slots = resp_x.shape[1]
    memory_head_number = prompt_keys.shape[2] // HDIM
    repeat = seq_count // memory_head_number
    shard_rows = prompt_keys.shape[1]
    spread_keys = jnp.repeat(
        prompt_keys.reshape(prompt_count, shard_rows, memory_head_number, HDIM), repeat, axis=2
    ).reshape(prompt_count, shard_rows, seq_count * HDIM)
    spread_values = jnp.repeat(
        prompt_values.reshape(prompt_count, shard_rows, memory_head_number, HDIM), repeat, axis=2
    ).reshape(prompt_count, shard_rows, seq_count * HDIM)
    moved_keys, moved_values = (
        lax.all_to_all(spread_keys, "seq", split_axis=2, concat_axis=1, tiled=True),
        lax.all_to_all(spread_values, "seq", split_axis=2, concat_axis=1, tiled=True),
    )
    resp_rates = lax.dynamic_slice_in_dim(ssm_rate, seq_index * resp_heads, resp_heads)
    resp_locals = []
    for item in range(responses_here):
        resp_locals.append(
            sequence_pass(resp_x[item], resp_dt[item], resp_b[item], resp_c[item], resp_rates)
        )
    prompt_rates = lax.dynamic_slice_in_dim(ssm_rate, resp_index * prompt_heads, prompt_heads)
    local_outs = []
    local_states = []
    prompt_decays = []
    log_totals = []
    for prompt in range(prompt_count):
        out, final, decays_to, total = sequence_pass(
            prompt_x[prompt], prompt_dt[prompt], prompt_b[prompt], prompt_c[prompt], prompt_rates
        )
        local_outs.append(out)
        local_states.append(final)
        prompt_decays.append(decays_to)
        log_totals.append(total)
    local_state = jnp.stack(local_states)
    decay_total = jnp.exp(jnp.stack(log_totals))
    identity = (jnp.ones_like(decay_total), jnp.zeros_like(local_state))

    def relay_step(element_tally, carry):
        sent = linkage_merge(carry, (decay_total, local_state))
        arrived = from_behind((sent[0], sent[1]), "seq", 1)
        first = seq_index == 0
        return (jnp.where(first, 1.0, arrived[0]), jnp.where(first, 0.0, arrived[1]))

    arriving_input = lax.fori_loop(0, seq_count - 1, relay_step, identity)
    prompt_outs = []
    for prompt in range(prompt_count):
        carried = jnp.einsum(
            "tn,hdn->thd",
            prompt_c[prompt].astype(jnp.float32),
            arriving_input[1][prompt],
            precision=lax.Precision.HIGHEST,
        )
        corrected = local_outs[prompt] + jnp.exp(prompt_decays[prompt]).T[:, :, None] * carried
        prompt_outs.append(head_norm(corrected).astype(jnp.bfloat16))
    prompt_ssm_out = jnp.stack(prompt_outs)
    inclusive = linkage_merge(arriving_input, (decay_total, local_state))[1]
    finals = broadcast(inclusive, "seq", seq_count - 1)
    ratio = seq_count // lax.axis_size("resp")
    piece = lax.dynamic_slice_in_dim(finals, seq_index % ratio * resp_heads, resp_heads, 1)
    start_states = broadcast(piece, "resp", seq_index // ratio)
    positions = lax.broadcasted_iota(jnp.int32, (slots,), 0)
    resp_outs = []
    for item in range(responses_here):
        out, final, decays_to, total = resp_locals[item]
        initial = lax.dynamic_index_in_dim(start_states, resp_group[item], 0, keepdims=False)
        carried = jnp.einsum(
            "tn,hdn->thd",
            resp_c[item].astype(jnp.float32),
            initial,
            precision=lax.Precision.HIGHEST,
        )
        corrected = out + jnp.exp(decays_to).T[:, :, None] * carried
        valid = positions < resp_len[item]
        resp_outs.append(jnp.where(valid[:, None], head_norm(corrected), 0.0).astype(jnp.bfloat16))
    resp_ssm_out = jnp.stack(resp_outs)
    heads_here = resp_query.shape[2] // HDIM
    own_head = seq_index // repeat
    own_keys = lax.dynamic_slice_in_dim(resp_keys, own_head * HDIM, HDIM, 2)
    own_values = lax.dynamic_slice_in_dim(resp_values, own_head * HDIM, HDIM, 2)
    prompt_len = moved_keys.shape[1]
    block = min(512, slots)
    scale = 1.0 / math.sqrt(HDIM)
    attn_outs = []
    for item in range(responses_here):
        group = resp_group[item]
        window_extent = resp_len[item]
        key_rows = jnp.concatenate(
            [lax.dynamic_index_in_dim(moved_keys, group, 0, keepdims=False), own_keys[item]], axis=0
        )
        value_rows = jnp.concatenate(
            [lax.dynamic_index_in_dim(moved_values, group, 0, keepdims=False), own_values[item]],
            axis=0,
        )
        queries = resp_query[item].reshape(slots * heads_here, HDIM)
        element_tally = key_rows.shape[0]

        def attend(start):
            rows = lax.dynamic_slice_in_dim(queries, start * heads_here, block * heads_here, 0)
            score = (
                lax.dot_general(
                    rows, key_rows, (((1,), (1,)), ((), ())), preferred_element_type=jnp.float32
                )
                * scale
            )
            position = (
                start + lax.broadcasted_iota(jnp.int32, (block * heads_here,), 0) // heads_here
            )
            column = lax.broadcasted_iota(jnp.int32, (1, element_tally), 1)
            allowed = (column < prompt_len) | (column - prompt_len <= position[:, None])
            score = jnp.where(allowed, score, -jnp.inf)
            top = jnp.max(score, axis=1, keepdims=True)
            raised = jnp.exp(score - top)
            total = jnp.sum(raised, axis=1, keepdims=True)
            weights = raised.astype(jnp.bfloat16)
            mixed = jnp.dot(weights, value_rows, preferred_element_type=jnp.float32) / total
            valid = position < window_extent
            return (
                jnp.where(valid[:, None], mixed, 0.0)
                .astype(jnp.bfloat16)
                .reshape(block, heads_here * HDIM)
            )

        def attend_block(start):
            return attend(start)

        starts = jnp.arange(slots // block, dtype=jnp.int32) * block
        attn_outs.append(lax.map(attend_block, starts).reshape(slots, heads_here * HDIM))
    resp_attn_out = jnp.stack(attn_outs)
    return (resp_attn_out, resp_ssm_out, prompt_ssm_out)


def solution(mesh):
    placed = (
        P(None, "seq", None),
        P(None, "seq", None),
        P("resp", None, "seq"),
        P("resp", None, None),
        P("resp", None, None),
        P(None, "seq", "resp"),
        P(None, "resp", "seq"),
        P(None, "seq", None),
        P(None, "seq", None),
        P("resp", None, "seq"),
        P("resp", "seq", None),
        P("resp", None, None),
        P("resp", None, None),
        P(),
        P("resp"),
        P("resp"),
    )
    return jax.shard_map(
        body,
        mesh=mesh,
        in_specs=placed,
        out_specs=(P("resp", None, "seq"), P("resp", None, "seq"), P(None, "seq", "resp")),
        check_vma=False,
    )
```

profile of v0, /device:TPU:33, one launch (start us, length us, event | category | flops | bytes accessed | tf_op | source)
XLA Modules:
  0.0 1405.0 jit_solution(7125134953789604929)
XLA Ops:
  26.9 735.4 %while.88 = (s32[]{:T(128)}, f32[2,32,64,128]{3,2,1,0:T(8,128)S(1)}, pred[]{:T(512)}, f32[2,32]{1,0:T(2,128)S(1)}, f32[2,32,64,128]{3,2,1,0:T(8,128)}, /*index=5*/s32[]{:T(128)}, s32[]{:T(128)}) while((s32[]{:T(128)}, f32[2,32,64,128]{3,2,1,0:T(8,128)S(1)}, pred[]{:T(512)}, f32[2,32]{1,0:T(2,128)S(1)}, ...), condition=%wide.region_14.15_spmd.clone, body=%wide.region_13.14_spmd.clone.sunk | while | flops 2097155 | bytes 27263388 | solution.py:147
  33.4 43.9 %collective-permute-done = f32[2,32,64,128]{3,2,1,0:T(8,128)S(1)} collective-permute-done((f32[2,32,64,128]{3,2,1,0:T(8,128)}, f32[2,32,64,128]{3,2,1,0:T(8,128)S(1)}, u32[]{:S(2)}, u32[]{:S(2)}) %collective-permute-start) | collective-permute-done | bytes 2097184 | tf_op jit(solution)/shard_map/while/body/eval_jaxpr/ppermute | solution.py:20
  87.7 42.9 %collective-permute-done = f32[2,32,64,128]{3,2,1,0:T(8,128)S(1)} collective-permute-done((f32[2,32,64,128]{3,2,1,0:T(8,128)}, f32[2,32,64,128]{3,2,1,0:T(8,128)S(1)}, u32[]{:S(2)}, u32[]{:S(2)}) %collective-permute-start) | collective-permute-done | bytes 2097184 | tf_op jit(solution)/shard_map/while/body/eval_jaxpr/ppermute | solution.py:20
  141.0 42.0 %collective-permute-done = f32[2,32,64,128]{3,2,1,0:T(8,128)S(1)} collective-permute-done((f32[2,32,64,128]{3,2,1,0:T(8,128)}, f32[2,32,64,128]{3,2,1,0:T(8,128)S(1)}, u32[]{:S(2)}, u32[]{:S(2)}) %collective-permute-start) | collective-permute-done | bytes 2097184 | tf_op jit(solution)/shard_map/while/body/eval_jaxpr/ppermute | solution.py:20
  193.4 41.1 %collective-permute-done = f32[2,32,64,128]{3,2,1,0:T(8,128)S(1)} collective-permute-done((f32[2,32,64,128]{3,2,1,0:T(8,128)}, f32[2,32,64,128]{3,2,1,0:T(8,128)S(1)}, u32[]{:S(2)}, u32[]{:S(2)}) %collective-permute-start) | collective-permute-done | bytes 2097184 | tf_op jit(solution)/shard_map/while/body/eval_jaxpr/ppermute | solution.py:20
  244.9 40.2 %collective-permute-done = f32[2,32,64,128]{3,2,1,0:T(8,128)S(1)} collective-permute-done((f32[2,32,64,128]{3,2,1,0:T(8,128)}, f32[2,32,64,128]{3,2,1,0:T(8,128)S(1)}, u32[]{:S(2)}, u32[]{:S(2)}) %collective-permute-start) | collective-permute-done | bytes 2097184 | tf_op jit(solution)/shard_map/while/body/eval_jaxpr/ppermute | solution.py:20
  296.6 39.2 %collective-permute-done = f32[2,32,64,128]{3,2,1,0:T(8,128)S(1)} collective-permute-done((f32[2,32,64,128]{3,2,1,0:T(8,128)}, f32[2,32,64,128]{3,2,1,0:T(8,128)S(1)}, u32[]{:S(2)}, u32[]{:S(2)}) %collective-permute-start) | collective-permute-done | bytes 2097184 | tf_op jit(solution)/shard_map/while/body/eval_jaxpr/ppermute | solution.py:20
  348.4 38.3 %collective-permute-done = f32[2,32,64,128]{3,2,1,0:T(8,128)S(1)} collective-permute-done((f32[2,32,64,128]{3,2,1,0:T(8,128)}, f32[2,32,64,128]{3,2,1,0:T(8,128)S(1)}, u32[]{:S(2)}, u32[]{:S(2)}) %collective-permute-start) | collective-permute-done | bytes 2097184 | tf_op jit(solution)/shard_map/while/body/eval_jaxpr/ppermute | solution.py:20
  399.2 37.4 %collective-permute-done = f32[2,32,64,128]{3,2,1,0:T(8,128)S(1)} collective-permute-done((f32[2,32,64,128]{3,2,1,0:T(8,128)}, f32[2,32,64,128]{3,2,1,0:T(8,128)S(1)}, u32[]{:S(2)}, u32[]{:S(2)}) %collective-permute-start) | collective-permute-done | bytes 2097184 | tf_op jit(solution)/shard_map/while/body/eval_jaxpr/ppermute | solution.py:20
  449.1 36.5 %collective-permute-done = f32[2,32,64,128]{3,2,1,0:T(8,128)S(1)} collective-permute-done((f32[2,32,64,128]{3,2,1,0:T(8,128)}, f32[2,32,64,128]{3,2,1,0:T(8,128)S(1)}, u32[]{:S(2)}, u32[]{:S(2)}) %collective-permute-start) | collective-permute-done | bytes 2097184 | tf_op jit(solution)/shard_map/while/body/eval_jaxpr/ppermute | solution.py:20
  498.1 35.6 %collective-permute-done = f32[2,32,64,128]{3,2,1,0:T(8,128)S(1)} collective-permute-done((f32[2,32,64,128]{3,2,1,0:T(8,128)}, f32[2,32,64,128]{3,2,1,0:T(8,128)S(1)}, u32[]{:S(2)}, u32[]{:S(2)}) %collective-permute-start) | collective-permute-done | bytes 2097184 | tf_op jit(solution)/shard_map/while/body/eval_jaxpr/ppermute | solution.py:20
  546.2 34.6 %collective-permute-done = f32[2,32,64,128]{3,2,1,0:T(8,128)S(1)} collective-permute-done((f32[2,32,64,128]{3,2,1,0:T(8,128)}, f32[2,32,64,128]{3,2,1,0:T(8,128)S(1)}, u32[]{:S(2)}, u32[]{:S(2)}) %collective-permute-start) | collective-permute-done | bytes 2097184 | tf_op jit(solution)/shard_map/while/body/eval_jaxpr/ppermute | solution.py:20
  593.3 33.7 %collective-permute-done = f32[2,32,64,128]{3,2,1,0:T(8,128)S(1)} collective-permute-done((f32[2,32,64,128]{3,2,1,0:T(8,128)}, f32[2,32,64,128]{3,2,1,0:T(8,128)S(1)}, u32[]{:S(2)}, u32[]{:S(2)}) %collective-permute-start) | collective-permute-done | bytes 2097184 | tf_op jit(solution)/shard_map/while/body/eval_jaxpr/ppermute | solution.py:20
  639.6 32.8 %collective-permute-done = f32[2,32,64,128]{3,2,1,0:T(8,128)S(1)} collective-permute-done((f32[2,32,64,128]{3,2,1,0:T(8,128)}, f32[2,32,64,128]{3,2,1,0:T(8,128)S(1)}, u32[]{:S(2)}, u32[]{:S(2)}) %collective-permute-start) | collective-permute-done | bytes 2097184 | tf_op jit(solution)/shard_map/while/body/eval_jaxpr/ppermute | solution.py:20
  684.9 31.9 %collective-permute-done = f32[2,32,64,128]{3,2,1,0:T(8,128)S(1)} collective-permute-done((f32[2,32,64,128]{3,2,1,0:T(8,128)}, f32[2,32,64,128]{3,2,1,0:T(8,128)S(1)}, u32[]{:S(2)}, u32[]{:S(2)}) %collective-permute-start) | collective-permute-done | bytes 2097184 | tf_op jit(solution)/shard_map/while/body/eval_jaxpr/ppermute | solution.py:20
  729.2 31.6 %collective-permute-done = f32[2,32,64,128]{3,2,1,0:T(8,128)S(1)} collective-permute-done((f32[2,32,64,128]{3,2,1,0:T(8,128)}, f32[2,32,64,128]{3,2,1,0:T(8,128)S(1)}, u32[]{:S(2)}, u32[]{:S(2)}) %collective-permute-start) | collective-permute-done | bytes 2097184 | tf_op jit(solution)/shard_map/while/body/eval_jaxpr/ppermute | solution.py:20
  793.5 185.1 %while.89 = (s32[]{:T(128)}, f32[16,64,128]{2,1,0:T(8,128)S(1)}, f32[16]{0:T(128)S(1)}, f32[8,128,16,64]{1,0,3,2:T(8,128)}, f32[8,16,128]{2,1,0:T(8,128)}, /*ind...) while((s32[]{:T(128)}, f32[16,64,128]{2,1,0:T(8,128)S(1)}, ...), condition=%wide.region_20.21_spmd.clone, body=%wide.region_18.20_spmd.clone.sunk | while | flops 275406880 | bytes 5156200 | solution.py:65
  801.7 14.3 %dynamic_update_slice.56 = f32[8,128,16,64]{1,0,3,2:T(8,128)} dynamic-update-slice(f32[8,128,16,64]{1,0,3,2:T(8,128)} %get-tuple-element.1050, f32[1,128,16,64]{1,0,3,2:T(1,128)} %bitcast.350, s32[]{:T(128)S(6)} %copy.140, s32[]{:T(128)} %constant.307.clone.1..sunk.4, s32[]{:T(128)} %constant.307.clone.1..sunk.4, s32[]{:T(128)} %constant.307.clone.1..sunk.4) | dynamic-update-slice | bytes 1048580 | tf_op jit(solution)/shard_map/while/body/jit(dynamic_update_index_in_dim)/dynamic_update_slice | solution.py:65
  824.9 14.3 %dynamic_update_slice.56 = f32[8,128,16,64]{1,0,3,2:T(8,128)} dynamic-update-slice(f32[8,128,16,64]{1,0,3,2:T(8,128)} %get-tuple-element.1050, f32[1,128,16,64]{1,0,3,2:T(1,128)} %bitcast.350, s32[]{:T(128)S(6)} %copy.140, s32[]{:T(128)} %constant.307.clone.1..sunk.4, s32[]{:T(128)} %constant.307.clone.1..sunk.4, s32[]{:T(128)} %constant.307.clone.1..sunk.4) | dynamic-update-slice | bytes 1048580 | tf_op jit(solution)/shard_map/while/body/jit(dynamic_update_index_in_dim)/dynamic_update_slice | solution.py:65
  871.2 14.3 %dynamic_update_slice.56 = f32[8,128,16,64]{1,0,3,2:T(8,128)} dynamic-update-slice(f32[8,128,16,64]{1,0,3,2:T(8,128)} %get-tuple-element.1050, f32[1,128,16,64]{1,0,3,2:T(1,128)} %bitcast.350, s32[]{:T(128)S(6)} %copy.140, s32[]{:T(128)} %constant.307.clone.1..sunk.4, s32[]{:T(128)} %constant.307.clone.1..sunk.4, s32[]{:T(128)} %constant.307.clone.1..sunk.4) | dynamic-update-slice | bytes 1048580 | tf_op jit(solution)/shard_map/while/body/jit(dynamic_update_index_in_dim)/dynamic_update_slice | solution.py:65
  995.3 178.4 %while.87 = (s32[]{:T(128)}, f32[16,64,128]{2,1,0:T(8,128)S(1)}, f32[16]{0:T(128)S(1)}, f32[8,128,16,64]{1,0,3,2:T(8,128)}, f32[8,16,128]{2,1,0:T(8,128)}, /*ind...) while((s32[]{:T(128)}, f32[16,64,128]{2,1,0:T(8,128)S(1)}, ...), condition=%wide.region_10.11_spmd.clone, body=%wide.region_8.10_spmd.clone.sunk | while | flops 275406880 | bytes 5156200 | solution.py:65
  1188.7 18.2 %all-to-all-start = ((bf16[2,128,2048]{1,0,2:T(2,128)(2,1)}), bf16[2,128,2048]{1,0,2:T(2,128)(2,1)S(1)}, u32[]{:S(2)}, u32[]{:S(2)}) async-start(bf16[2,128,2048]{1,0,2:T(2,128)(2,1)} %bitcast.4), calls=%async_computation | async-start | bytes 2097152 | tf_op jit(solution)/shard_map/all_to_all | solution.py:115
  1235.5 59.7 %while.86 = (s32[]{:T(128)}, bf16[2,512,512]{2,1,0:T(8,128)(2,1)S(1)}, s32[2]{0:T(128)S(1)}, s32[]{:T(128)}, bf16[4096,128]{1,0:T(8,128)(2,1)}, /*index=5*/bf16[...) while((s32[]{:T(128)}, ...), condition=%wide.region_7.8_spmd, body=%wide.region_4.7_spmd.sunk | while | flops 3329007616 | bytes 83501280 | solution.py:230
  1302.0 60.1 %while.85 = (s32[]{:T(128)}, bf16[2,512,512]{2,1,0:T(8,128)(2,1)S(1)}, s32[2]{0:T(128)S(1)}, s32[]{:T(128)}, bf16[4096,128]{1,0:T(8,128)(2,1)}, /*index=5*/bf16[...) while((s32[]{:T(128)}, ...), condition=%wide.region_3.4_spmd, body=%wide.region_0.3_spmd.sunk | while | flops 3329007616 | bytes 83501280 | solution.py:230
  (509 shorter events, 759.5 us)
Async XLA Ops:
  10.3 1176.6 %all-to-all-start.1 = ((bf16[2,128,2048]{1,0,2:T(2,128)(2,1)}), bf16[2,128,2048]{1,0,2:T(2,128)(2,1)}, u32[]{:S(2)}, u32[]{:S(2)}) async-start(bf16[2,128,2048]{1,0,2:T(2,128)(2,1)} %bitcast.12), calls=%async_computation.1 | async-start | bytes 2097152 | tf_op jit(solution)/shard_map/all_to_all | solution.py:116
  17.2 1282.4 %all-reduce.3.cloned.1.call-start = ((), (), s32[]{:S(2)}) async-start(), calls=%async_computation.2 | async-start | bytes 4194304 | tf_op jit(solution)/shard_map/psum | solution.py:25
  30.1 47.2 %collective-permute-start = (f32[2,32,64,128]{3,2,1,0:T(8,128)}, f32[2,32,64,128]{3,2,1,0:T(8,128)S(1)}, u32[]{:S(2)}, u32[]{:S(2)}) collective-permute-start(f32[2,32,64,128]{3,2,1,0:T(8,128)} %fusion.258), channel_id=1, source_target_pairs={{0,8},{8,16},{16,24},{24,32},{32,40},{40,48},{48,56},{56,64},{64,7... | collective-permute-start | bytes 6291464 | tf_op jit(solution)/shard_map/while/body/eval_jaxpr/ppermute | solution.py:20
  81.9 48.6 %collective-permute-start = (f32[2,32,64,128]{3,2,1,0:T(8,128)}, f32[2,32,64,128]{3,2,1,0:T(8,128)S(1)}, u32[]{:S(2)}, u32[]{:S(2)}) collective-permute-start(f32[2,32,64,128]{3,2,1,0:T(8,128)} %fusion.258), channel_id=1, source_target_pairs={{0,8},{8,16},{16,24},{24,32},{32,40},{40,48},{48,56},{56,64},{64,7... | collective-permute-start | bytes 6291464 | tf_op jit(solution)/shard_map/while/body/eval_jaxpr/ppermute | solution.py:20
  135.3 47.7 %collective-permute-start = (f32[2,32,64,128]{3,2,1,0:T(8,128)}, f32[2,32,64,128]{3,2,1,0:T(8,128)S(1)}, u32[]{:S(2)}, u32[]{:S(2)}) collective-permute-start(f32[2,32,64,128]{3,2,1,0:T(8,128)} %fusion.258), channel_id=1, source_target_pairs={{0,8},{8,16},{16,24},{24,32},{32,40},{40,48},{48,56},{56,64},{64,7... | collective-permute-start | bytes 6291464 | tf_op jit(solution)/shard_map/while/body/eval_jaxpr/ppermute | solution.py:20
  187.7 46.8 %collective-permute-start = (f32[2,32,64,128]{3,2,1,0:T(8,128)}, f32[2,32,64,128]{3,2,1,0:T(8,128)S(1)}, u32[]{:S(2)}, u32[]{:S(2)}) collective-permute-start(f32[2,32,64,128]{3,2,1,0:T(8,128)} %fusion.258), channel_id=1, source_target_pairs={{0,8},{8,16},{16,24},{24,32},{32,40},{40,48},{48,56},{56,64},{64,7... | collective-permute-start | bytes 6291464 | tf_op jit(solution)/shard_map/while/body/eval_jaxpr/ppermute | solution.py:20
  239.2 45.9 %collective-permute-start = (f32[2,32,64,128]{3,2,1,0:T(8,128)}, f32[2,32,64,128]{3,2,1,0:T(8,128)S(1)}, u32[]{:S(2)}, u32[]{:S(2)}) collective-permute-start(f32[2,32,64,128]{3,2,1,0:T(8,128)} %fusion.258), channel_id=1, source_target_pairs={{0,8},{8,16},{16,24},{24,32},{32,40},{40,48},{48,56},{56,64},{64,7... | collective-permute-start | bytes 6291464 | tf_op jit(solution)/shard_map/while/body/eval_jaxpr/ppermute | solution.py:20
  289.8 46.1 %collective-permute-start = (f32[2,32,64,128]{3,2,1,0:T(8,128)}, f32[2,32,64,128]{3,2,1,0:T(8,128)S(1)}, u32[]{:S(2)}, u32[]{:S(2)}) collective-permute-start(f32[2,32,64,128]{3,2,1,0:T(8,128)} %fusion.258), channel_id=1, source_target_pairs={{0,8},{8,16},{16,24},{24,32},{32,40},{40,48},{48,56},{56,64},{64,7... | collective-permute-start | bytes 6291464 | tf_op jit(solution)/shard_map/while/body/eval_jaxpr/ppermute | solution.py:20
  340.6 46.1 %collective-permute-start = (f32[2,32,64,128]{3,2,1,0:T(8,128)}, f32[2,32,64,128]{3,2,1,0:T(8,128)S(1)}, u32[]{:S(2)}, u32[]{:S(2)}) collective-permute-start(f32[2,32,64,128]{3,2,1,0:T(8,128)} %fusion.258), channel_id=1, source_target_pairs={{0,8},{8,16},{16,24},{24,32},{32,40},{40,48},{48,56},{56,64},{64,7... | collective-permute-start | bytes 6291464 | tf_op jit(solution)/shard_map/while/body/eval_jaxpr/ppermute | solution.py:20
  391.4 45.2 %collective-permute-start = (f32[2,32,64,128]{3,2,1,0:T(8,128)}, f32[2,32,64,128]{3,2,1,0:T(8,128)S(1)}, u32[]{:S(2)}, u32[]{:S(2)}) collective-permute-start(f32[2,32,64,128]{3,2,1,0:T(8,128)} %fusion.258), channel_id=1, source_target_pairs={{0,8},{8,16},{16,24},{24,32},{32,40},{40,48},{48,56},{56,64},{64,7... | collective-permute-start | bytes 6291464 | tf_op jit(solution)/shard_map/while/body/eval_jaxpr/ppermute | solution.py:20
  441.3 44.3 %collective-permute-start = (f32[2,32,64,128]{3,2,1,0:T(8,128)}, f32[2,32,64,128]{3,2,1,0:T(8,128)S(1)}, u32[]{:S(2)}, u32[]{:S(2)}) collective-permute-start(f32[2,32,64,128]{3,2,1,0:T(8,128)} %fusion.258), channel_id=1, source_target_pairs={{0,8},{8,16},{16,24},{24,32},{32,40},{40,48},{48,56},{56,64},{64,7... | collective-permute-start | bytes 6291464 | tf_op jit(solution)/shard_map/while/body/eval_jaxpr/ppermute | solution.py:20
  490.3 43.4 %collective-permute-start = (f32[2,32,64,128]{3,2,1,0:T(8,128)}, f32[2,32,64,128]{3,2,1,0:T(8,128)S(1)}, u32[]{:S(2)}, u32[]{:S(2)}) collective-permute-start(f32[2,32,64,128]{3,2,1,0:T(8,128)} %fusion.258), channel_id=1, source_target_pairs={{0,8},{8,16},{16,24},{24,32},{32,40},{40,48},{48,56},{56,64},{64,7... | collective-permute-start | bytes 6291464 | tf_op jit(solution)/shard_map/while/body/eval_jaxpr/ppermute | solution.py:20
  538.4 42.5 %collective-permute-start = (f32[2,32,64,128]{3,2,1,0:T(8,128)}, f32[2,32,64,128]{3,2,1,0:T(8,128)S(1)}, u32[]{:S(2)}, u32[]{:S(2)}) collective-permute-start(f32[2,32,64,128]{3,2,1,0:T(8,128)} %fusion.258), channel_id=1, source_target_pairs={{0,8},{8,16},{16,24},{24,32},{32,40},{40,48},{48,56},{56,64},{64,7... | collective-permute-start | bytes 6291464 | tf_op jit(solution)/shard_map/while/body/eval_jaxpr/ppermute | solution.py:20
  585.5 41.5 %collective-permute-start = (f32[2,32,64,128]{3,2,1,0:T(8,128)}, f32[2,32,64,128]{3,2,1,0:T(8,128)S(1)}, u32[]{:S(2)}, u32[]{:S(2)}) collective-permute-start(f32[2,32,64,128]{3,2,1,0:T(8,128)} %fusion.258), channel_id=1, source_target_pairs={{0,8},{8,16},{16,24},{24,32},{32,40},{40,48},{48,56},{56,64},{64,7... | collective-permute-start | bytes 6291464 | tf_op jit(solution)/shard_map/while/body/eval_jaxpr/ppermute | solution.py:20
  631.7 40.6 %collective-permute-start = (f32[2,32,64,128]{3,2,1,0:T(8,128)}, f32[2,32,64,128]{3,2,1,0:T(8,128)S(1)}, u32[]{:S(2)}, u32[]{:S(2)}) collective-permute-start(f32[2,32,64,128]{3,2,1,0:T(8,128)} %fusion.258), channel_id=1, source_target_pairs={{0,8},{8,16},{16,24},{24,32},{32,40},{40,48},{48,56},{56,64},{64,7... | collective-permute-start | bytes 6291464 | tf_op jit(solution)/shard_map/while/body/eval_jaxpr/ppermute | solution.py:20
  677.0 39.7 %collective-permute-start = (f32[2,32,64,128]{3,2,1,0:T(8,128)}, f32[2,32,64,128]{3,2,1,0:T(8,128)S(1)}, u32[]{:S(2)}, u32[]{:S(2)}) collective-permute-start(f32[2,32,64,128]{3,2,1,0:T(8,128)} %fusion.258), channel_id=1, source_target_pairs={{0,8},{8,16},{16,24},{24,32},{32,40},{40,48},{48,56},{56,64},{64,7... | collective-permute-start | bytes 6291464 | tf_op jit(solution)/shard_map/while/body/eval_jaxpr/ppermute | solution.py:20
  721.4 39.4 %collective-permute-start = (f32[2,32,64,128]{3,2,1,0:T(8,128)}, f32[2,32,64,128]{3,2,1,0:T(8,128)S(1)}, u32[]{:S(2)}, u32[]{:S(2)}) collective-permute-start(f32[2,32,64,128]{3,2,1,0:T(8,128)} %fusion.258), channel_id=1, source_target_pairs={{0,8},{8,16},{16,24},{24,32},{32,40},{40,48},{48,56},{56,64},{64,7... | collective-permute-start | bytes 6291464 | tf_op jit(solution)/shard_map/while/body/eval_jaxpr/ppermute | solution.py:20
  995.3 178.4 %copy-start.28 = (f32[32,128]{1,0:T(8,128)S(1)}, f32[32,128]{1,0:T(8,128)}, u32[]{:S(2)}) copy-start(f32[32,128]{1,0:T(8,128)} %copy-done.27) | copy-start | bytes 49156
  995.3 180.8 %copy-start.16 = (bf16[2,128,128]{2,1,0:T(8,128)(2,1)S(1)}, bf16[2,128,128]{2,1,0:T(8,128)(2,1)}, u32[]{:S(2)}) copy-start(bf16[2,128,128]{2,1,0:T(8,128)(2,1)} %param.34) | copy-start | bytes 196612
  995.3 180.8 %copy-start.24 = (f32[128,32]{0,1:T(8,128)S(1)}, f32[128,32]{0,1:T(8,128)}, u32[]{:S(2)}) copy-start(f32[128,32]{0,1:T(8,128)} %get-tuple-element.681) | copy-start | bytes 49156
  1188.7 42.8 %all-to-all-start = ((bf16[2,128,2048]{1,0,2:T(2,128)(2,1)}), bf16[2,128,2048]{1,0,2:T(2,128)(2,1)S(1)}, u32[]{:S(2)}, u32[]{:S(2)}) async-start(bf16[2,128,2048]{1,0,2:T(2,128)(2,1)} %bitcast.4), calls=%async_computation | async-start | bytes 2097152 | tf_op jit(solution)/shard_map/all_to_all | solution.py:115
  1206.9 170.3 %all-reduce.5.cloned.1.call-start = ((), (), s32[]{:S(2)}) async-start(), calls=%async_computation.3 | async-start | bytes 2097152 | tf_op jit(solution)/shard_map/psum | solution.py:25
  1235.5 62.2 %copy-start.4 = (bf16[2048,128]{1,0:T(8,128)(2,1)S(1)}, bf16[2048,128]{1,0:T(8,128)(2,1)}, u32[]{:S(2)}) copy-start(bf16[2048,128]{1,0:T(8,128)(2,1)} %get-tuple-element.665) | copy-start | bytes 1572868
  1362.2 15.0 %copy-start.5 = (bf16[2,1024,128]{2,1,0:T(8,128)(2,1)S(1)}, bf16[2,1024,128]{2,1,0:T(8,128)(2,1)}, u32[]{:S(2)}) copy-start(bf16[2,1024,128]{2,1,0:T(8,128)(2,1)} %param.38) | copy-start | bytes 1572868
  (52 other events, 230.7 us)
Sparse Core Ops, SparseCore 0:
  765.4 116.5 all-reduce.2
  1302.1 75.0 all-reduce.4
where the time goes:
time: 1430 us; the launch traced here: 1400 us
  waiting for transfers between devices  574 us (40%)
  local copies, waits for them, and re-layouts  350 us (24%)
  matrix products  185 us (13%)
  other arithmetic  145 us (10%)
  starting transfers between devices  129 us (9%)
  between operations  18.5 us (1%)
    ppermute x15, waiting for transfers between devices, from_behind(): return lax.ppermute(block, axis, route)  562 us
    dynamic_update_slice x16, local copies, waits for them, and re-layouts, sequence_pass(): lax.scan(advance, start, (xs, ss, bs, cs))  228 us
    ppermute x15, starting transfers between devices, from_behind(): return lax.ppermute(block, axis, route)  103 us
    add x15, other arithmetic, linkage_merge(): later[0][:, :, None, None] * earlier[1] + later[1]  47.7 us
    dot_general x18, matrix products, block_pass(): jnp.einsum('hts,shp->thp', mixing, inputs, preferred_element_type=jnp.flo...  40.3 us
    reduce_sum x4, other arithmetic, attend(): total = jnp.sum(raised, axis=1, keepdims=True)  38.9 us
    dot_general x4, matrix products, attend(): jnp.dot(weights, value_rows, preferred_element_type=jnp.float32) / total  36.9 us
    dot_general x18, matrix products, block_pass(): jnp.einsum('tn,hpn->thp', c_rows.astype(jnp.float32), state, precision=la...  30.8 us
  transfers between devices with their start and end apart: 19, of which 16 were waited for; matrix products, arithmetic and copies ran while one was open for 45% of the time, Pallas kernels for 0%

commit v1 on v0

--- a/solution.py
+++ b/solution.py
@@ -136,28 +136,30 @@
         log_totals.append(total)
     local_state = jnp.stack(local_states)
     decay_total = jnp.exp(jnp.stack(log_totals))
-    identity = (jnp.ones_like(decay_total), jnp.zeros_like(local_state))
-
-    def relay_step(element_tally, carry):
-        sent = linkage_merge(carry, (decay_total, local_state))
-        arrived = from_behind((sent[0], sent[1]), "seq", 1)
-        first = seq_index == 0
-        return (jnp.where(first, 1.0, arrived[0]), jnp.where(first, 0.0, arrived[1]))
-
-    arriving_input = lax.fori_loop(0, seq_count - 1, relay_step, identity)
+    gathered_states = lax.all_gather(local_state, "seq")
+    gathered_decays = lax.all_gather(decay_total, "seq")
+    shard = lax.broadcasted_iota(jnp.int32, (seq_count, seq_count), 0)
+    later = lax.broadcasted_iota(jnp.int32, (seq_count, seq_count), 1)
+    between = (later > shard) & (later < seq_index)
+    after = later > shard
+    factors = gathered_decays[None]
+    before_weights = jnp.prod(jnp.where(between[:, :, None, None], factors, 1.0), axis=1)
+    before_weights = jnp.where((shard[:, 0] < seq_index)[:, None, None], before_weights, 0.0)
+    final_weights = jnp.prod(jnp.where(after[:, :, None, None], factors, 1.0), axis=1)
+    arriving_state = jnp.sum(before_weights[:, :, :, None, None] * gathered_states, axis=0)
+    inclusive = jnp.sum(final_weights[:, :, :, None, None] * gathered_states, axis=0)
     prompt_outs = []
     for prompt in range(prompt_count):
         carried = jnp.einsum(
             "tn,hdn->thd",
             prompt_c[prompt].astype(jnp.float32),
-            arriving_input[1][prompt],
+            arriving_state[prompt],
             precision=lax.Precision.HIGHEST,
         )
         corrected = local_outs[prompt] + jnp.exp(prompt_decays[prompt]).T[:, :, None] * carried
         prompt_outs.append(head_norm(corrected).astype(jnp.bfloat16))
     prompt_ssm_out = jnp.stack(prompt_outs)
-    inclusive = linkage_merge(arriving_input, (decay_total, local_state))[1]
-    finals = broadcast(inclusive, "seq", seq_count - 1)
+    finals = inclusive
     ratio = seq_count // lax.axis_size("resp")
     piece = lax.dynamic_slice_in_dim(finals, seq_index % ratio * resp_heads, resp_heads, 1)
     start_states = broadcast(piece, "resp", seq_index // ratio)

time: 1430 us -> 718 us (0.50)
  waiting for transfers between devices: 574 us -> 60.8 us
  starting transfers between devices: 129 us -> 21.9 us
  other arithmetic: 145 us -> 95.9 us
  local copies, waits for them, and re-layouts: 350 us -> 319 us
  blocking collectives: 0 us -> 27.3 us
  matrix products: 185 us -> 158 us
    ppermute x15 -> x0, waiting for transfers between devices: 562 us -> none  [from_behind(): return lax.ppermute(block, axis, route)]
    ppermute x15 -> x0, starting transfers between devices: 103 us -> none  [from_behind(): return lax.ppermute(block, axis, route)]
    psum x2 -> x1, waiting for transfers between devices: 12.2 us -> 60.7 us  [broadcast(): return lax.psum(kept, axis)]
    add x15 -> x0, other arithmetic: 47.7 us -> none  [linkage_merge(): later[0][:, :, None, None] * earlier[1] + later[1]]
    all_gather x0 -> x1, blocking collectives: none -> 27.3 us  [body(): gathered_decays = lax.all_gather(decay_total, 'seq')]
    while x38 -> x8, local copies, waits for them, and re-layouts: 19.8 us -> 0.02 us
    dot_general x18, matrix products: 30.8 us -> 15.6 us  [block_pass(): jnp.einsum('tn,hpn->thp', c_rows.astype(jnp.float32), state, precision=la...]
  transfers between devices with their start and end apart: 19 -> 4, of which waited for: 16 -> 1; matrix products, arithmetic and copies ran while one was open for 45% -> 75% of each run, Pallas kernels for 0% -> 0%
where the time goes in v1:
time: 718 us; the launch traced here: 706 us
  local copies, waits for them, and re-layouts  319 us (44%)
  matrix products  158 us (22%)
  other arithmetic  95.9 us (13%)
  waiting for transfers between devices  60.8 us (8%)
  blocking collectives  27.3 us (4%)
  starting transfers between devices  21.9 us (3%)
  between operations  18.8 us (3%)
    dynamic_update_slice x16, local copies, waits for them, and re-layouts, sequence_pass(): lax.scan(advance, start, (xs, ss, bs, cs))  228 us
    psum x1, waiting for transfers between devices, broadcast(): return lax.psum(kept, axis)  60.7 us
    reduce_sum x4, other arithmetic, attend(): total = jnp.sum(raised, axis=1, keepdims=True)  38.9 us
    dot_general x4, matrix products, attend(): jnp.dot(weights, value_rows, preferred_element_type=jnp.float32) / total  36.9 us
    dot_general x4, matrix products, attend(): lax.dot_general(rows, key_rows, (((1,), (1,)), ((), ())), preferred_eleme...  29.8 us
    dot_general x18, matrix products, block_pass(): jnp.einsum('hts,shp->thp', mixing, inputs, preferred_element_type=jnp.flo...  27.7 us
    all_gather x1, blocking collectives, body(): gathered_decays = lax.all_gather(decay_total, 'seq')  27.3 us
    dot_general x18, matrix products, block_pass(): jnp.einsum('thp,tn->hpn', weighted, b_rows, preferred_element_type=jnp.fl...  19.6 us
  transfers between devices with their start and end apart: 4, of which 1 were waited for; matrix products, arithmetic and copies ran while one was open for 75% of the time, Pallas kernels for 0%

profile of v1, /device:TPU:33, one launch (start us, length us, event | category | flops | bytes accessed | tf_op | source)
XLA Modules:
  0.0 705.9 jit_solution(6514653137282749298)
XLA Ops:
  27.7 27.3 %all_gather.10 = f32[16,2,32]{2,1,0:T(2,128)S(1)} all-gather(f32[1,2,32]{2,1,0:T(2,128)S(1)} %maximum_exponential_fusion), channel_id=1, replica_groups=mesh['seq'=16,'resp'=8] {'seq'}, dimensions={0}, use_global_device_ids=true | all-gather | bytes 4352 | tf_op jit(solution)/shard_map/all_gather | solution.py:140
  97.9 165.2 %while.74 = (s32[]{:T(128)}, f32[16,64,128]{2,1,0:T(8,128)S(1)}, f32[16]{0:T(128)S(1)}, f32[8,128,16,64]{1,0,3,2:T(8,128)}, f32[8,16,128]{2,1,0:T(8,128)S(1)}, /...) while((s32[]{:T(128)}, f32[16,64,128]{2,1,0:T(8,128)S(1)}, ...), condition=%wide.region_10.11_spmd.clone, body=%wide.region_8.10_spmd.clone.sunk | while | flops 275406880 | bytes 5157145 | solution.py:65
  103.1 14.3 %dynamic_update_slice.54 = f32[8,128,16,64]{1,0,3,2:T(8,128)} dynamic-update-slice(f32[8,128,16,64]{1,0,3,2:T(8,128)} %get-tuple-element.994, f32[1,128,16,64]{1,0,3,2:T(1,128)S(1)} %bitcast.353, s32[]{:T(128)} %get-tuple-element.991, s32[]{:T(128)} %constant.290.clone.1..sunk.2, s32[]{:T(128)} %constant.290.clone.1..sunk.2, s32[]{:T(128)} %constant.290.clone.1..sunk.2) | dynamic-update-slice | bytes 1048580 | tf_op jit(solution)/shard_map/while/body/jit(dynamic_update_index_in_dim)/dynamic_update_slice | solution.py:65
  123.8 14.3 %dynamic_update_slice.54 = f32[8,128,16,64]{1,0,3,2:T(8,128)} dynamic-update-slice(f32[8,128,16,64]{1,0,3,2:T(8,128)} %get-tuple-element.994, f32[1,128,16,64]{1,0,3,2:T(1,128)S(1)} %bitcast.353, s32[]{:T(128)} %get-tuple-element.991, s32[]{:T(128)} %constant.290.clone.1..sunk.2, s32[]{:T(128)} %constant.290.clone.1..sunk.2, s32[]{:T(128)} %constant.290.clone.1..sunk.2) | dynamic-update-slice | bytes 1048580 | tf_op jit(solution)/shard_map/while/body/jit(dynamic_update_index_in_dim)/dynamic_update_slice | solution.py:65
  144.4 14.3 %dynamic_update_slice.54 = f32[8,128,16,64]{1,0,3,2:T(8,128)} dynamic-update-slice(f32[8,128,16,64]{1,0,3,2:T(8,128)} %get-tuple-element.994, f32[1,128,16,64]{1,0,3,2:T(1,128)S(1)} %bitcast.353, s32[]{:T(128)} %get-tuple-element.991, s32[]{:T(128)} %constant.290.clone.1..sunk.2, s32[]{:T(128)} %constant.290.clone.1..sunk.2, s32[]{:T(128)} %constant.290.clone.1..sunk.2) | dynamic-update-slice | bytes 1048580 | tf_op jit(solution)/shard_map/while/body/jit(dynamic_update_index_in_dim)/dynamic_update_slice | solution.py:65
  165.1 14.3 %dynamic_update_slice.54 = f32[8,128,16,64]{1,0,3,2:T(8,128)} dynamic-update-slice(f32[8,128,16,64]{1,0,3,2:T(8,128)} %get-tuple-element.994, f32[1,128,16,64]{1,0,3,2:T(1,128)S(1)} %bitcast.353, s32[]{:T(128)} %get-tuple-element.991, s32[]{:T(128)} %constant.290.clone.1..sunk.2, s32[]{:T(128)} %constant.290.clone.1..sunk.2, s32[]{:T(128)} %constant.290.clone.1..sunk.2) | dynamic-update-slice | bytes 1048580 | tf_op jit(solution)/shard_map/while/body/jit(dynamic_update_index_in_dim)/dynamic_update_slice | solution.py:65
  185.8 14.2 %dynamic_update_slice.54 = f32[8,128,16,64]{1,0,3,2:T(8,128)} dynamic-update-slice(f32[8,128,16,64]{1,0,3,2:T(8,128)} %get-tuple-element.994, f32[1,128,16,64]{1,0,3,2:T(1,128)S(1)} %bitcast.353, s32[]{:T(128)} %get-tuple-element.991, s32[]{:T(128)} %constant.290.clone.1..sunk.2, s32[]{:T(128)} %constant.290.clone.1..sunk.2, s32[]{:T(128)} %constant.290.clone.1..sunk.2) | dynamic-update-slice | bytes 1048580 | tf_op jit(solution)/shard_map/while/body/jit(dynamic_update_index_in_dim)/dynamic_update_slice | solution.py:65
  206.4 14.2 %dynamic_update_slice.54 = f32[8,128,16,64]{1,0,3,2:T(8,128)} dynamic-update-slice(f32[8,128,16,64]{1,0,3,2:T(8,128)} %get-tuple-element.994, f32[1,128,16,64]{1,0,3,2:T(1,128)S(1)} %bitcast.353, s32[]{:T(128)} %get-tuple-element.991, s32[]{:T(128)} %constant.290.clone.1..sunk.2, s32[]{:T(128)} %constant.290.clone.1..sunk.2, s32[]{:T(128)} %constant.290.clone.1..sunk.2) | dynamic-update-slice | bytes 1048580 | tf_op jit(solution)/shard_map/while/body/jit(dynamic_update_index_in_dim)/dynamic_update_slice | solution.py:65
  227.0 14.2 %dynamic_update_slice.54 = f32[8,128,16,64]{1,0,3,2:T(8,128)} dynamic-update-slice(f32[8,128,16,64]{1,0,3,2:T(8,128)} %get-tuple-element.994, f32[1,128,16,64]{1,0,3,2:T(1,128)S(1)} %bitcast.353, s32[]{:T(128)} %get-tuple-element.991, s32[]{:T(128)} %constant.290.clone.1..sunk.2, s32[]{:T(128)} %constant.290.clone.1..sunk.2, s32[]{:T(128)} %constant.290.clone.1..sunk.2) | dynamic-update-slice | bytes 1048580 | tf_op jit(solution)/shard_map/while/body/jit(dynamic_update_index_in_dim)/dynamic_update_slice | solution.py:65
  247.6 14.2 %dynamic_update_slice.54 = f32[8,128,16,64]{1,0,3,2:T(8,128)} dynamic-update-slice(f32[8,128,16,64]{1,0,3,2:T(8,128)} %get-tuple-element.994, f32[1,128,16,64]{1,0,3,2:T(1,128)S(1)} %bitcast.353, s32[]{:T(128)} %get-tuple-element.991, s32[]{:T(128)} %constant.290.clone.1..sunk.2, s32[]{:T(128)} %constant.290.clone.1..sunk.2, s32[]{:T(128)} %constant.290.clone.1..sunk.2) | dynamic-update-slice | bytes 1048580 | tf_op jit(solution)/shard_map/while/body/jit(dynamic_update_index_in_dim)/dynamic_update_slice | solution.py:65
  266.3 151.9 %while.75 = (s32[]{:T(128)}, f32[16,64,128]{2,1,0:T(8,128)S(1)}, f32[16]{0:T(128)S(1)}, f32[8,128,16,64]{1,0,3,2:T(8,128)}, f32[8,16,128]{2,1,0:T(8,128)S(1)}, /...) while((s32[]{:T(128)}, f32[16,64,128]{2,1,0:T(8,128)S(1)}, ...), condition=%wide.region_19.20_spmd.clone, body=%wide.region_17.19_spmd.clone.sunk | while | flops 275406880 | bytes 5156637 | solution.py:65
  269.8 14.2 %dynamic_update_slice.56 = f32[8,128,16,64]{1,0,3,2:T(8,128)} dynamic-update-slice(f32[8,128,16,64]{1,0,3,2:T(8,128)} %get-tuple-element.955, f32[1,128,16,64]{1,0,3,2:T(1,128)S(1)} %bitcast.354, s32[]{:T(128)} %get-tuple-element.952, s32[]{:T(128)} %constant.290.clone.1..sunk.3, s32[]{:T(128)} %constant.290.clone.1..sunk.3, s32[]{:T(128)} %constant.290.clone.1..sunk.3) | dynamic-update-slice | bytes 1048580 | tf_op jit(solution)/shard_map/while/body/jit(dynamic_update_index_in_dim)/dynamic_update_slice | solution.py:65
  288.8 14.2 %dynamic_update_slice.56 = f32[8,128,16,64]{1,0,3,2:T(8,128)} dynamic-update-slice(f32[8,128,16,64]{1,0,3,2:T(8,128)} %get-tuple-element.955, f32[1,128,16,64]{1,0,3,2:T(1,128)S(1)} %bitcast.354, s32[]{:T(128)} %get-tuple-element.952, s32[]{:T(128)} %constant.290.clone.1..sunk.3, s32[]{:T(128)} %constant.290.clone.1..sunk.3, s32[]{:T(128)} %constant.290.clone.1..sunk.3) | dynamic-update-slice | bytes 1048580 | tf_op jit(solution)/shard_map/while/body/jit(dynamic_update_index_in_dim)/dynamic_update_slice | solution.py:65
  307.8 14.2 %dynamic_update_slice.56 = f32[8,128,16,64]{1,0,3,2:T(8,128)} dynamic-update-slice(f32[8,128,16,64]{1,0,3,2:T(8,128)} %get-tuple-element.955, f32[1,128,16,64]{1,0,3,2:T(1,128)S(1)} %bitcast.354, s32[]{:T(128)} %get-tuple-element.952, s32[]{:T(128)} %constant.290.clone.1..sunk.3, s32[]{:T(128)} %constant.290.clone.1..sunk.3, s32[]{:T(128)} %constant.290.clone.1..sunk.3) | dynamic-update-slice | bytes 1048580 | tf_op jit(solution)/shard_map/while/body/jit(dynamic_update_index_in_dim)/dynamic_update_slice | solution.py:65
  326.8 14.2 %dynamic_update_slice.56 = f32[8,128,16,64]{1,0,3,2:T(8,128)} dynamic-update-slice(f32[8,128,16,64]{1,0,3,2:T(8,128)} %get-tuple-element.955, f32[1,128,16,64]{1,0,3,2:T(1,128)S(1)} %bitcast.354, s32[]{:T(128)} %get-tuple-element.952, s32[]{:T(128)} %constant.290.clone.1..sunk.3, s32[]{:T(128)} %constant.290.clone.1..sunk.3, s32[]{:T(128)} %constant.290.clone.1..sunk.3) | dynamic-update-slice | bytes 1048580 | tf_op jit(solution)/shard_map/while/body/jit(dynamic_update_index_in_dim)/dynamic_update_slice | solution.py:65
  345.8 14.2 %dynamic_update_slice.56 = f32[8,128,16,64]{1,0,3,2:T(8,128)} dynamic-update-slice(f32[8,128,16,64]{1,0,3,2:T(8,128)} %get-tuple-element.955, f32[1,128,16,64]{1,0,3,2:T(1,128)S(1)} %bitcast.354, s32[]{:T(128)} %get-tuple-element.952, s32[]{:T(128)} %constant.290.clone.1..sunk.3, s32[]{:T(128)} %constant.290.clone.1..sunk.3, s32[]{:T(128)} %constant.290.clone.1..sunk.3) | dynamic-update-slice | bytes 1048580 | tf_op jit(solution)/shard_map/while/body/jit(dynamic_update_index_in_dim)/dynamic_update_slice | solution.py:65
  364.8 14.2 %dynamic_update_slice.56 = f32[8,128,16,64]{1,0,3,2:T(8,128)} dynamic-update-slice(f32[8,128,16,64]{1,0,3,2:T(8,128)} %get-tuple-element.955, f32[1,128,16,64]{1,0,3,2:T(1,128)S(1)} %bitcast.354, s32[]{:T(128)} %get-tuple-element.952, s32[]{:T(128)} %constant.290.clone.1..sunk.3, s32[]{:T(128)} %constant.290.clone.1..sunk.3, s32[]{:T(128)} %constant.290.clone.1..sunk.3) | dynamic-update-slice | bytes 1048580 | tf_op jit(solution)/shard_map/while/body/jit(dynamic_update_index_in_dim)/dynamic_update_slice | solution.py:65
  383.7 14.2 %dynamic_update_slice.56 = f32[8,128,16,64]{1,0,3,2:T(8,128)} dynamic-update-slice(f32[8,128,16,64]{1,0,3,2:T(8,128)} %get-tuple-element.955, f32[1,128,16,64]{1,0,3,2:T(1,128)S(1)} %bitcast.354, s32[]{:T(128)} %get-tuple-element.952, s32[]{:T(128)} %constant.290.clone.1..sunk.3, s32[]{:T(128)} %constant.290.clone.1..sunk.3, s32[]{:T(128)} %constant.290.clone.1..sunk.3) | dynamic-update-slice | bytes 1048580 | tf_op jit(solution)/shard_map/while/body/jit(dynamic_update_index_in_dim)/dynamic_update_slice | solution.py:65
  402.7 14.2 %dynamic_update_slice.56 = f32[8,128,16,64]{1,0,3,2:T(8,128)} dynamic-update-slice(f32[8,128,16,64]{1,0,3,2:T(8,128)} %get-tuple-element.955, f32[1,128,16,64]{1,0,3,2:T(1,128)S(1)} %bitcast.354, s32[]{:T(128)} %get-tuple-element.952, s32[]{:T(128)} %constant.290.clone.1..sunk.3, s32[]{:T(128)} %constant.290.clone.1..sunk.3, s32[]{:T(128)} %constant.290.clone.1..sunk.3) | dynamic-update-slice | bytes 1048580 | tf_op jit(solution)/shard_map/while/body/jit(dynamic_update_index_in_dim)/dynamic_update_slice | solution.py:65
  428.0 10.6 %all-reduce.2.cloned.1.call-start = ((), (), s32[]{:S(2)}) async-start(), calls=%async_computation.2 | async-start | bytes 2097152 | tf_op jit(solution)/shard_map/psum | solution.py:25
  471.0 61.3 %while.72 = (s32[]{:T(128)}, bf16[2,512,512]{2,1,0:T(8,128)(2,1)}, s32[2]{0:T(128)S(1)}, s32[]{:T(128)}, bf16[4096,128]{1,0:T(8,128)(2,1)S(1)}, /*index=5*/bf16[...) while((s32[]{:T(128)}, bf16[2,512,512]{2,1,0:T(8,128)(2,1)}, ...), condition=%wide.region_3.4_spmd, body=%wide.region_0.3_spmd.sunk | while | flops 3329007616 | bytes 83501776 | solution.py:232
  532.3 60.7 %while.73 = (s32[]{:T(128)}, bf16[2,512,512]{2,1,0:T(8,128)(2,1)S(1)}, s32[2]{0:T(128)S(1)}, s32[]{:T(128)}, bf16[4096,128]{1,0:T(8,128)(2,1)}, /*index=5*/bf16[...) while((s32[]{:T(128)}, ...), condition=%wide.region_7.8_spmd, body=%wide.region_4.7_spmd.sunk | while | flops 3329007616 | bytes 83501264 | solution.py:232
  595.8 13.8 %multiply_reduce_fusion = (f32[2,32,64,128]{3,2,1,0:T(8,128)S(1)}, f32[2,32,64,128]{3,2,1,0:T(8,128)S(1)}) fusion(f32[16,2,32,64,128]{4,3,2,1,0:T(8,128)} %bitcast.355, f32[16,2,32]{2,1,0:T(2,128)S(1)} %copy-done.33, f32[16,2,32]{2,1,0:T(2,128)S(1)} %copy-done.32), kind=kLoop, calls=%fused_computation.140 | loop fusion | flops 32505856 | bytes 37756928 | tf_op jit(solution)/shard_map/reduce_sum | solution.py:149
  617.3 60.7 %all-reduce.2.cloned.1.call-done = f32[2,16,64,128]{3,2,1,0:T(8,128)} async-done(((f32[2,16,64,128]{3,2,1,0:T(8,128)}), f32[2,16,64,128]{3,2,1,0:T(8,128)}) %all-reduce.2.cloned.1.call-update) | async-done | bytes 1048592 | tf_op jit(solution)/shard_map/psum | solution.py:25
  (438 shorter events, 342.9 us)
Async XLA Ops:
  7.2 588.6 %all-gather.3.cloned.1.call-start = ((), (), s32[]{:S(2)}) async-start(), calls=%async_computation.3 | async-start | bytes 35651584 | tf_op jit(solution)/shard_map/all_gather | solution.py:139
  11.1 449.7 %copy-start.24 = (f32[128,32]{0,1:T(8,128)}, f32[128,32]{0,1:T(8,128)S(1)}, u32[]{:S(2)}) copy-start(f32[128,32]{0,1:T(8,128)S(1)} %get-tuple-element.615) | copy-start | bytes 49156
  15.3 9.7 %copy-start.20 = (f32[2,32,128]{2,1,0:T(8,128)S(1)}, f32[2,32,128]{2,1,0:T(8,128)}, u32[]{:S(2)}) copy-start(f32[2,32,128]{2,1,0:T(8,128)} %param.30) | copy-start | bytes 98308
  15.3 10.9 %copy-start.16 = (bf16[2,128,128]{2,1,0:T(8,128)(2,1)S(1)}, bf16[2,128,128]{2,1,0:T(8,128)(2,1)}, u32[]{:S(2)}) copy-start(bf16[2,128,128]{2,1,0:T(8,128)(2,1)} %param.32) | copy-start | bytes 196612
  15.3 40.9 %copy-start.46 = (f32[256]{0:T(256)S(1)}, f32[256]{0:T(256)}, u32[]{:S(2)}) copy-start(f32[256]{0:T(256)} %param.37) | copy-start | bytes 3076
  17.5 404.1 %all-to-all-start.1 = ((bf16[2,128,2048]{1,0,2:T(2,128)(2,1)}), bf16[2,128,2048]{1,0,2:T(2,128)(2,1)}, u32[]{:S(2)}, u32[]{:S(2)}) async-start(bf16[2,128,2048]{1,0,2:T(2,128)(2,1)} %bitcast.12), calls=%async_computation.1 | async-start | bytes 2097152 | tf_op jit(solution)/shard_map/all_to_all | solution.py:116
  86.1 8.6 %copy-start.41 = (pred[16,16]{1,0:T(8,128)(4,1)S(1)}, pred[16,16]{1,0:T(8,128)(4,1)}, u32[]{:S(2)}) copy-start(pred[16,16]{1,0:T(8,128)(4,1)} %get-tuple-element.635) | copy-start | bytes 772
  86.1 8.6 %copy-start.42 = (pred[16,16]{1,0:T(8,128)(4,1)S(1)}, pred[16,16]{1,0:T(8,128)(4,1)}, u32[]{:S(2)}) copy-start(pred[16,16]{1,0:T(8,128)(4,1)} %get-tuple-element.636) | copy-start | bytes 772
  266.2 152.0 %copy-start.45 = (pred[16]{0:T(512)(128)(4,1)S(1)}, pred[16]{0:T(512)(128)(4,1)}, u32[]{:S(2)}) copy-start(pred[16]{0:T(512)(128)(4,1)} %compare_bitcast_fusion) | copy-start | bytes 52
  266.3 153.3 %copy-start.8 = (bf16[1,128,2048]{1,2,0:T(8,128)(2,1)S(1)}, bf16[1,128,2048]{1,2,0:T(8,128)(2,1)}, u32[]{:S(2)}) copy-start(bf16[1,128,2048]{1,2,0:T(8,128)(2,1)} %copy-done.7) | copy-start | bytes 1572868
  266.3 153.3 %copy-start.31 = (f32[32,128]{1,0:T(8,128)S(1)}, f32[32,128]{1,0:T(8,128)}, u32[]{:S(2)}) copy-start(f32[32,128]{1,0:T(8,128)} %copy-done.30) | copy-start | bytes 49156
  266.3 153.3 %copy-start.34 = (f32[128,128]{1,0:T(8,128)S(1)}, f32[128,128]{1,0:T(8,128)}, u32[]{:S(2)}) copy-start(f32[128,128]{1,0:T(8,128)} %fusion.150) | copy-start | bytes 196612
  266.3 153.3 %copy-start.37 = (pred[128,128]{1,0:T(8,128)(4,1)S(1)}, pred[128,128]{1,0:T(8,128)(4,1)}, u32[]{:S(2)}) copy-start(pred[128,128]{1,0:T(8,128)(4,1)} %iota_compare_fusion.4) | copy-start | bytes 49156
  266.3 153.3 %copy-start.38 = (f32[32,128]{1,0:T(8,128)S(1)}, f32[32,128]{1,0:T(8,128)}, u32[]{:S(2)}) copy-start(f32[32,128]{1,0:T(8,128)} %get-tuple-element.611) | copy-start | bytes 49156
  423.5 40.9 %all-to-all-start = ((bf16[2,128,2048]{1,0,2:T(2,128)(2,1)}), bf16[2,128,2048]{1,0,2:T(2,128)(2,1)S(1)}, u32[]{:S(2)}, u32[]{:S(2)}) async-start(bf16[2,128,2048]{1,0,2:T(2,128)(2,1)} %bitcast.4), calls=%async_computation | async-start | bytes 2097152 | tf_op jit(solution)/shard_map/all_to_all | solution.py:115
  428.0 250.1 %all-reduce.2.cloned.1.call-start = ((), (), s32[]{:S(2)}) async-start(), calls=%async_computation.2 | async-start | bytes 2097152 | tf_op jit(solution)/shard_map/psum | solution.py:25
  480.3 11.0 %copy-start.15 = (bf16[3072,128]{1,0:T(8,128)(2,1)S(1)}, bf16[3072,128]{1,0:T(8,128)(2,1)}, u32[]{:S(2)}) copy-start(bf16[3072,128]{1,0:T(8,128)(2,1)} %get-tuple-element.934) | copy-start | bytes 2359300 | tf_op jit(solution)/shard_map/while
  510.9 11.0 %copy-start.15 = (bf16[3072,128]{1,0:T(8,128)(2,1)S(1)}, bf16[3072,128]{1,0:T(8,128)(2,1)}, u32[]{:S(2)}) copy-start(bf16[3072,128]{1,0:T(8,128)(2,1)} %get-tuple-element.934) | copy-start | bytes 2359300 | tf_op jit(solution)/shard_map/while
  542.2 11.1 %copy-start.14 = (bf16[3072,128]{1,0:T(8,128)(2,1)S(1)}, bf16[3072,128]{1,0:T(8,128)(2,1)}, u32[]{:S(2)}) copy-start(bf16[3072,128]{1,0:T(8,128)(2,1)} %get-tuple-element.901) | copy-start | bytes 2359300 | tf_op jit(solution)/shard_map/while
  572.3 11.1 %copy-start.14 = (bf16[3072,128]{1,0:T(8,128)(2,1)S(1)}, bf16[3072,128]{1,0:T(8,128)(2,1)}, u32[]{:S(2)}) copy-start(bf16[3072,128]{1,0:T(8,128)(2,1)} %get-tuple-element.901) | copy-start | bytes 2359300 | tf_op jit(solution)/shard_map/while
  595.8 14.9 %copy-start.17 = (bf16[2,128,128]{2,1,0:T(8,128)(2,1)S(1)}, bf16[2,128,128]{2,1,0:T(8,128)(2,1)}, u32[]{:S(2)}) copy-start(bf16[2,128,128]{2,1,0:T(8,128)(2,1)} %param.32) | copy-start | bytes 196612
  595.8 14.9 %copy-start.27 = (f32[128,32]{0,1:T(8,128)S(1)}, f32[128,32]{0,1:T(8,128)}, u32[]{:S(2)}) copy-start(f32[128,32]{0,1:T(8,128)} %get-tuple-element.616) | copy-start | bytes 49156
  614.3 63.7 %copy-start.2 = (bf16[2,1024,128]{2,1,0:T(8,128)(2,1)S(1)}, bf16[2,1024,128]{2,1,0:T(8,128)(2,1)}, u32[]{:S(2)}) copy-start(bf16[2,1024,128]{2,1,0:T(8,128)(2,1)} %param.36) | copy-start | bytes 1572868
  614.3 63.7 %copy-start.21 = (f32[1024,16]{0,1:T(8,128)S(1)}, f32[1024,16]{0,1:T(8,128)}, u32[]{:S(2)}) copy-start(f32[1024,16]{0,1:T(8,128)} %bitcast_bitcast_fusion.1) | copy-start | bytes 196612
  (29 other events, 113.2 us)
Sparse Core Ops, SparseCore 0:
  15.5 205.0 all-gather.2
  610.9 67.1 all-reduce.1
